TPU v7x, 512 devices: a whole 4x4x16 slice. The times are simulated.
512 devices in a mesh: img: 128 (over y, z_lo, x), vol: 4 (over z_hi, core).
Axes of the slice: x: 4, y: 4, z: 16 (z_hi: 2, z_lo: 8; z = z_hi * 8 + z_lo), core: 2. Of those that a mesh axis runs over, the one named last changes fastest.
Arguments:
- images: bfloat16 [128, 400, 400], P('img'), may hold values from -6 to 6
- volume: bfloat16 [4, 32768, 400], P('vol', 'img'), may hold values from -6 to 6
- row_order: int32 [128, 8, 400], P('img'), may hold values from 0 to 399, each once within a row
- tap_owner: int32 [4, 128, 8, 200, 1], P('vol', 'img'), may hold values from 0 to 127; in each aligned block of 1600 rows (0 to 1599, 1600 to 3199, ..., all dimensions but the last counted through in order) at most 17 rows name the same one
- tap_local: int32 [4, 128, 8, 200], P('vol', 'img'), may hold values from 0 to 255
- interp_index: int32 [4, 128, 8, 100], P('vol', 'img'), may hold values from 0 to 63
- interp_table: float32 [64], replicated, may hold values from 0 to 1
- ctf_index: int32 [128], P('img'), may hold values from 0 to 15
- ctf_defocus: float32 [16], replicated, may hold values from 2.5e-05 to 0.00025
- ctf_phase: float32 [16], replicated, may hold values from 0 to 1.2
- noise_inv: float32 [128], P('img'), may hold values from 0.5 to 4
Outputs:
- data_sum: float32 [4, 32768, 400], P('vol', 'img')
- weight_sum: float32 [4, 32768, 200], P('vol', 'img')
- pose_weights: float32 [128, 8], P('img')
Inputs may be any that keep to these rules, and one draw needn't show every extreme that they name: `tap_owner`: in each aligned block of 1600 tap rows (one block per slab and image shard), no owner is named more than 17 times.
All inputs are finite; a program needn't handle non-finite values.
Results may differ from a plain program's by a relative error of at most 0.007.
Values may be sent and summed in bfloat16 or wider, within the bound.
No kernel may reach another device: no remote copies, remote signals or barrier semaphores. Data moves between devices by JAX's collectives and lax.ppermute only.
A program may use at most 128 MiB of HBM per device.

v0:
```python
import math

import jax
import jax.numpy as jnp
from jax import lax
from jax.sharding import PartitionSpec as P


def fourier_tables(size_k, size_f):
    positions = jnp.arange(size_k, dtype=jnp.int32)
    columns = jnp.arange(size_f, dtype=jnp.int32)
    scale_factor = 1.0 / math.sqrt(size_k)
    phase_x = (positions[:, None] * columns[None, :] % size_k).astype(jnp.float32) * (
        2.0 * math.pi / size_k
    )
    table_x = jnp.concatenate([jnp.cos(phase_x), -jnp.sin(phase_x)], axis=1) * scale_factor
    phase_y = (positions[:, None] * positions[None, :] % size_k).astype(jnp.float32) * (
        2.0 * math.pi / size_k
    )
    table_y = jnp.concatenate([jnp.cos(phase_y), jnp.sin(phase_y)], axis=1) * scale_factor
    return (table_x.astype(jnp.bfloat16), table_y.astype(jnp.bfloat16))


def contrast_of(radius_sq, defocus, phase_shift, size_f):
    columns = jnp.arange(size_f, dtype=jnp.int32)
    radius = radius_sq[..., None] + columns * columns
    return -jnp.sin(defocus * radius.astype(jnp.float32) + phase_shift)


def half_transform(images, table_x):
    return jnp.einsum("iyx,xc->iyc", images, table_x, preferred_element_type=jnp.float32).astype(
        jnp.bfloat16
    )


def full_transform(half_spec, table_y, width):
    other = jnp.concatenate([half_spec[..., width:], -half_spec[..., :width]], axis=-1)
    stacked = jnp.concatenate([half_spec, other], axis=1)
    return jnp.einsum("uy,iyc->iuc", table_y, stacked, preferred_element_type=jnp.float32).astype(
        jnp.bfloat16
    )


def small_lookup(index_rows, table):
    entries = jnp.arange(table.shape[0], dtype=jnp.int32)
    return jnp.sum(
        jnp.where(index_rows[..., None] == entries, table, jnp.zeros_like(table)), axis=-1
    )


def one_hot(index, count):
    return (index[..., None] == jnp.arange(count, dtype=jnp.int32)).astype(jnp.bfloat16)


def exchange(rows, main_count, over_count):
    peers = rows.shape[0] // (main_count + over_count)
    width = rows.shape[1]
    main = rows[: peers * main_count].reshape(peers, main_count, width)
    spare = -(-width * over_count // main_count)
    over = rows[peers * main_count :].reshape(peers, over_count * width)
    over = jnp.pad(over, ((0, 0), (0, spare * main_count - over_count * width)))
    packed = jnp.concatenate([main, over.reshape(peers, main_count, spare)], axis=2)
    moved = lax.all_to_all(packed, "img", split_axis=0, concat_axis=0, tiled=True)
    got_main = moved[:, :, :width].reshape(peers * main_count, width)
    got_over = moved[:, :, width:].reshape(peers, main_count * spare)[:, : over_count * width]
    return jnp.concatenate([got_main, got_over.reshape(peers * over_count, width)], axis=0)


def body(
    images,
    volume,
    row_order,
    tap_owner,
    tap_local,
    interp_index,
    interp_table,
    ctf_index,
    ctf_defocus,
    ctf_phase,
    noise_inv,
):
    f32, bf16, i32 = jnp.float32, jnp.bfloat16, jnp.int32
    image_count, size_k, _ = images.shape
    size_f = size_k // 2
    width = 2 * size_f
    pose_count = row_order.shape[1]
    vol_count = lax.axis_size("vol")
    img_count = lax.axis_size("img")
    quarter = size_k // vol_count
    slab_rows = volume.shape[1]
    slab_index = lax.axis_index("vol")
    row_count = image_count * pose_count * quarter

    table_x, table_y = fourier_tables(size_k, size_f)
    half_spec = half_transform(images, table_x)
    spectrum = full_transform(half_spec, table_y, size_f)
    freq_rows = lax.dynamic_slice_in_dim(row_order, slab_index * quarter, quarter, 2)
    spec_rows = jnp.einsum(
        "ipqu,iuc->ipqc", one_hot(freq_rows, size_k), spectrum, preferred_element_type=f32
    ).astype(bf16).reshape(row_count, width)

    owners = tap_owner[0, ..., 0].reshape(-1)
    local_rows = tap_local[0].reshape(-1)
    request_count = owners.shape[0]
    capacity = request_count * 6 // (5 * img_count) + 2
    slot_count = img_count * capacity
    owner_hot = one_hot(owners, img_count)
    order = jnp.arange(request_count, dtype=i32)
    before = (order[None, :] < order[:, None]).astype(bf16)
    earlier = jnp.dot(before, owner_hot, preferred_element_type=f32)
    rank = jnp.sum(earlier * owner_hot.astype(f32), axis=1).astype(i32)
    main_count = 16
    over_count = capacity - main_count
    slot_of = jnp.where(
        rank < main_count,
        owners * main_count + rank,
        img_count * main_count + owners * over_count + rank - main_count,
    )
    slot_pair = slot_of.reshape(row_count, 2)
    slots = jnp.arange(slot_count, dtype=i32)
    pick_even = (slot_pair[:, 0:1] == slots[None, :]).astype(bf16)
    pick_odd = (slot_pair[:, 1:2] == slots[None, :]).astype(bf16)
    slot_hot_t = (slots[:, None] == slot_of[None, :]).astype(bf16)
    row_of_slot = (
        (slots[:, None] == slot_pair[None, :, 0]) | (slots[:, None] == slot_pair[None, :, 1])
    ).astype(bf16)

    signed_abs = jnp.where(freq_rows < size_f, freq_rows, size_k - freq_rows)
    shape4 = (image_count, pose_count, quarter, 2)
    per_row = lambda a: jnp.broadcast_to(a.reshape(image_count, pose_count, quarter, 1), shape4)
    pose_ids = jnp.broadcast_to(jnp.arange(pose_count, dtype=i32)[None, :, None, None], shape4)
    tap_ids = jnp.broadcast_to(jnp.arange(2, dtype=i32)[None, None, None, :], shape4)
    image_ids = jnp.broadcast_to(jnp.arange(image_count, dtype=i32)[:, None, None, None], shape4)
    ctf_ids = jnp.broadcast_to(ctf_index[:, None, None, None], shape4)
    meta = jnp.stack(
        [
            local_rows.reshape(shape4),
            per_row(signed_abs),
            pose_ids,
            per_row(interp_index[0]),
            tap_ids,
            jnp.ones_like(tap_ids),
            ctf_ids,
            image_ids,
        ],
        axis=-1,
    ).reshape(request_count, -1).astype(bf16)
    meta_count = meta.shape[1]
    send_spec = jnp.dot(row_of_slot, spec_rows, preferred_element_type=f32).astype(bf16)
    send_meta = jnp.dot(slot_hot_t, meta, preferred_element_type=f32).astype(bf16)
    got_both = exchange(jnp.concatenate([send_spec, send_meta], axis=1), main_count, over_count)
    got_spec = got_both[:, :width]
    got = got_both[:, width:].astype(f32).astype(i32)

    got_local, got_abs, got_pose, got_interp = got[:, 0], got[:, 1], got[:, 2], got[:, 3]
    got_tap, got_valid, got_ctf, got_image = got[:, 4], got[:, 5], got[:, 6], got[:, 7]
    row_hot = one_hot(jnp.where(got_valid > 0, got_local, slab_rows), slab_rows)
    found = jnp.dot(row_hot, volume[0], preferred_element_type=f32).astype(bf16)
    returned = exchange(found, main_count, over_count)

    defocus = small_lookup(ctf_index, ctf_defocus)[:, None, None, None]
    phase_shift = small_lookup(ctf_index, ctf_phase)[:, None, None, None]
    contrast = contrast_of(signed_abs * signed_abs, defocus, phase_shift, size_f).reshape(
        row_count, size_f
    )
    got_contrast = contrast_of(
        got_abs * got_abs,
        small_lookup(got_ctf, ctf_defocus)[:, None],
        small_lookup(got_ctf, ctf_phase)[:, None],
        size_f,
    )
    returned, contrast, got_contrast = lax.optimization_barrier((returned, contrast, got_contrast))

    tap_even = jnp.dot(pick_even, returned, preferred_element_type=f32).astype(bf16).astype(f32)
    tap_odd = jnp.dot(pick_odd, returned, preferred_element_type=f32).astype(bf16).astype(f32)
    mixing = small_lookup(interp_index[0], interp_table).reshape(row_count, 1)
    sliced = mixing * tap_even + (1.0 - mixing) * tap_odd
    spec_float = spec_rows.astype(f32)
    cross_term = contrast * (
        spec_float[:, :size_f] * sliced[:, :size_f] + spec_float[:, size_f:] * sliced[:, size_f:]
    )
    power_term = contrast * contrast * (sliced[:, :size_f] ** 2 + sliced[:, size_f:] ** 2)
    partial_value = jnp.sum(
        (cross_term - 0.5 * power_term).reshape(image_count, pose_count, quarter * size_f), axis=-1
    )
    score_sum = lax.psum(partial_value, "vol")
    scores = noise_inv[:, None] * score_sum * (1.0 / math.sqrt(size_k * size_f))
    pose_weights = jax.nn.softmax(scores, axis=-1)

    by_peer = lax.all_to_all(
        jnp.broadcast_to(pose_weights.reshape(1, 1, -1), (img_count, 1, image_count * pose_count)),
        "img",
        split_axis=0,
        concat_axis=0,
        tiled=True,
    )
    combo = got_image * pose_count + got_pose
    combo_ids = jnp.arange(image_count * pose_count, dtype=i32)
    main_slots = img_count * main_count

    def weight_by_peer(picked, per_peer):
        picked = picked.reshape(img_count, per_peer)
        return jnp.sum(
            jnp.where(picked[..., None] == combo_ids, by_peer, 0.0), axis=-1
        ).reshape(-1)

    weight_of = jnp.concatenate(
        [
            weight_by_peer(combo[:main_slots], main_count),
            weight_by_peer(combo[main_slots:], over_count),
        ]
    )
    mix_of = small_lookup(got_interp, interp_table)
    mix_k = jnp.where(got_tap == 0, mix_of, 1.0 - mix_of)
    coef = mix_k * weight_of
    scaled = coef[:, None] * got_contrast
    got_float = got_spec.astype(f32)
    data_rows = (jnp.concatenate([scaled, scaled], axis=-1) * got_float).astype(bf16)
    weight_rows = (scaled * got_contrast).astype(bf16)
    data_acc = jnp.einsum("sr,sw->rw", row_hot, data_rows, preferred_element_type=f32)
    weight_acc = jnp.einsum("sr,sw->rw", row_hot, weight_rows, preferred_element_type=f32)
    return (data_acc[None], weight_acc[None], pose_weights)


def solution(mesh):
    placed = (
        P("img", None, None),
        P("vol", "img", None),
        P("img", None, None),
        P("vol", "img", None, None, None),
        P("vol", "img", None, None),
        P("vol", "img", None, None),
        P(),
        P("img"),
        P(),
        P(),
        P("img"),
    )
    return jax.shard_map(
        body,
        mesh=mesh,
        in_specs=placed,
        out_specs=(P("vol", "img", None), P("vol", "img", None), P("img", None)),
        check_vma=False,
    )
```

profile of v0, /device:TPU:6, one launch (start us, length us, event | category | flops | bytes accessed | tf_op | source)
XLA Modules:
  0.0 332.2 jit_solution(9603536456960087790)
XLA Ops:
  0.6 0.8 multiply_reduce_fusion
  1.5 1.8 fusion.27
  3.4 3.0 sine_negate_fusion.2
  6.4 3.3 fusion.46
  10.7 0.2 stack_broadcast_in_dim.46
  10.9 0.8 fusion.82
  11.7 0.2 stack_broadcast_in_dim.41
  11.9 0.2 stack_broadcast_in_dim.42
  12.1 0.2 stack_broadcast_in_dim.44
  12.4 0.2 stack_broadcast_in_dim.48
  12.6 0.4 convert_element_type.116
  13.4 0.4 slice_reduce_fusion.4
  13.9 0.5 copy-done.8
  14.5 0.8 fusion.28
  15.3 2.0 fusion.24
  17.3 1.4 copy.53
  18.6 0.6 reshape.294
  19.4 2.5 fusion.16
  21.9 2.7 fusion.9
  24.6 1.4 fusion.21
  26.1 0.5 copy.55
  26.5 2.8 copy.54
  29.3 0.4 pad_maximum_fusion.2
  29.7 116.4 %all_to_all.15 = bf16[128,16,434]{2,1,0:T(8,128)(2,1)S(1)} all-to-all(bf16[128,16,434]{2,1,0:T(8,128)(2,1)S(1)} %pad_maximum_fusion.2), channel_id=1, replica_groups=mesh['img'=128,'vol'=4] {'img'}, dimensions={0} | all-to-all | bytes 3555328 | tf_op jit(solution)/shard_map/all_to_all | solution.py:63
  146.1 0.2 slice.133
  146.3 0.5 reshape.305
  146.8 0.6 copy-done.1
  147.4 1.3 convert_convert_fusion
  148.7 3.8 %slice_reduce_fusion.1 = (s32[2176]{0:T(1024)S(1)}, s32[2176]{0:T(1024)S(1)}, s32[2176]{0:T(1024)S(1)}, s32[2176]{0:T(1024)S(1)}, s32[2176,1]{1,0:T(8,128)}) fusion(s32[2176,8]{1,0:T(8,128)S(1)} %convert_convert_fusion), kind=kLoop, calls=%fused_computation.59 | loop fusion | flops 10880 | bytes 104448 | tf_op jit(solution)/shard_map/slice | solution.py:155
  152.5 0.8 convolution_convert_fusion
  153.3 0.2 slice.142
  153.5 1.2 copy.62
  154.8 2.4 copy.61
  157.2 3.5 %pad_maximum_fusion.3 = bf16[128,16,425]{2,1,0:T(8,128)(2,1)} fusion(bf16[128,16,25]{2,1,0:T(8,128)(2,1)} %copy.62, bf16[128,16,400]{2,1,0:T(8,128)(2,1)} %bitcast.67), kind=kLoop, calls=%fused_computation.31 | loop fusion | flops 3481600 | bytes 3481600 | tf_op jit(solution)/shard_map/concatenate | solution.py:62
  160.7 10.0 %all-to-all-start.1 = ((bf16[128,16,425]{2,1,0:T(8,128)(2,1)}), bf16[128,16,425]{2,1,0:T(8,128)(2,1)}, u32[]{:S(2)}, u32[]{:S(2)}) async-start(bf16[128,16,425]{2,1,0:T(8,128)(2,1)} %pad_maximum_fusion.3), calls=%async_computation.1 | async-start | bytes 4194304 | tf_op jit(solution)/shard_map/all_to_all | solution.py:63
  170.8 1.2 convert_element_type.135
  172.9 0.7 fusion.85
  173.6 4.7 %sine_negate_fusion.1 = f32[800,200]{0,1:T(8,128)} fusion(f32[]{:T(128)} %get-tuple-element.29, s32[200]{0:T(256)S(1)} %iota_multiply_fusion, s32[800]{0:T(1024)S(1)} %add.153, f32[]{:T(128)} %get-tuple-element.28), kind=kLoop, calls=%fused_computation.94 | loop fusion | flops 800000 | bytes 644008 | tf_op jit(solution)/shard_map/neg | solution.py:27
  178.3 1.6 slice_reduce_fusion.2
  180.0 1.0 slice_reduce_fusion.5
  181.3 9.3 %sine_negate_fusion = f32[2176,200]{1,0:T(8,128)} fusion(f32[2176]{0:T(1024)S(1)} %get-tuple-element.16, s32[200]{0:T(256)S(1)} %iota_multiply_fusion, s32[2176]{0:T(1024)S(1)} %get-tuple-element.10, f32[2176]{0:T(1024)S(1)} %get-tuple-element.15), kind=kLoop, calls=%fused_computation.26 | loop fusion | flops 2176000 | bytes 1767712 | tf_op jit(solution)/shard_map/neg | solution.py:27
  190.6 76.0 %all-to-all-done.1 = bf16[128,16,425]{2,1,0:T(8,128)(2,1)} async-done(((bf16[128,16,425]{2,1,0:T(8,128)(2,1)}), bf16[128,16,425]{2,1,0:T(8,128)(2,1)}, u32[]{:S(2)}, u32[]{:S(2)}) %all-to-all-start.1) | async-done | bytes 1740832 | tf_op jit(solution)/shard_map/all_to_all | solution.py:63
  266.6 1.2 slice.145
  267.9 1.2 reshape.306
  269.0 2.0 pad_maximum_fusion.1
  271.0 2.2 fusion.25
  273.3 2.3 multiply_add_fusion
  275.5 0.3 fusion.56
  276.0 18.7 %psum.7 = f32[1,8]{1,0:T(1,128)S(1)} all-reduce(f32[1,8]{1,0:T(1,128)S(1)} %bitcast.73), channel_id=1, replica_groups=mesh['img'=128,'vol'=4] {'vol'}, use_global_device_ids=true, to_apply=%region_9.10 | all-reduce | flops 8 | bytes 64 | tf_op jit(solution)/shard_map/psum | solution.py:186
  294.7 0.6 fusion.97
  295.3 1.3 fusion.98
  296.6 0.6 fusion.104
  297.2 0.7 broadcast_in_dim.123
  297.9 9.7 %all-to-all-start.2 = ((f32[128,1,8]{2,1,0:T(1,128)}), f32[128,1,8]{2,1,0:T(1,128)S(1)}, u32[]{:S(2)}, u32[]{:S(2)}) async-start(f32[128,1,8]{2,1,0:T(1,128)} %broadcast_in_dim.123), calls=%async_computation.2 | async-start | bytes 131072 | tf_op jit(solution)/shard_map/all_to_all | solution.py:190
  307.6 1.1 broadcast_divide_fusion
  308.8 12.1 %all-to-all-done.2 = f32[128,1,8]{2,1,0:T(1,128)S(1)} async-done(((f32[128,1,8]{2,1,0:T(1,128)}), f32[128,1,8]{2,1,0:T(1,128)S(1)}, u32[]{:S(2)}, u32[]{:S(2)}) %all-to-all-start.2) | async-done | bytes 4128 | tf_op jit(solution)/shard_map/all_to_all | solution.py:190
  321.2 1.8 fusion.81
  323.0 0.4 copy.67
  323.4 1.0 fusion.35
  324.4 0.7 copy-done.3
  325.1 2.1 fusion.33
  327.2 0.4 broadcast_multiply_fusion
  327.5 1.2 copy-done.2
  328.7 3.2 fusion.30
  (65 shorter events, 2.5 us)
Async XLA Ops:
  0.6 13.3 %copy-start = (bf16[1,400,400]{2,1,0:T(8,128)(2,1)S(1)}, bf16[1,400,400]{2,1,0:T(8,128)(2,1)}, u32[]{:S(2)}) copy-start(bf16[1,400,400]{2,1,0:T(8,128)(2,1)} %param.11) | copy-start | bytes 960004
  3.3 7.1 %copy-start.11 = (s32[1,1,8,100]{3,2,1,0:T(8,128)S(1)}, s32[1,1,8,100]{3,2,1,0:T(8,128)}, u32[]{:S(2)}) copy-start(s32[1,1,8,100]{3,2,1,0:T(8,128)} %param.16) | copy-start | bytes 9604
  3.3 7.1 %copy-start.12 = (s32[1,1,8,200]{3,2,1,0:T(8,128)S(1)}, s32[1,1,8,200]{3,2,1,0:T(8,128)}, u32[]{:S(2)}) copy-start(s32[1,1,8,200]{3,2,1,0:T(8,128)} %param.15) | copy-start | bytes 19204
  13.3 1.0 copy-start.8
  13.4 1.1 copy-start.9
  19.3 2.7 copy-start.5
  146.1 1.3 copy-start.1
  146.8 5.7 %copy-start.6 = (bf16[128,416]{1,0:T(8,128)(2,1)}, bf16[128,416]{1,0:T(8,128)(2,1)S(1)}, u32[]{:S(2)}) copy-start(bf16[128,416]{1,0:T(8,128)(2,1)S(1)} %reshape.305) | copy-start | bytes 319492
  148.7 3.8 %copy-start.10 = (bf16[1,256,400]{1,2,0:T(8,128)(2,1)S(1)}, bf16[1,256,400]{1,2,0:T(8,128)(2,1)}, u32[]{:S(2)}) copy-start(bf16[1,256,400]{1,2,0:T(8,128)(2,1)} %param.12) | copy-start | bytes 614404
  160.7 105.9 %all-to-all-start.1 = ((bf16[128,16,425]{2,1,0:T(8,128)(2,1)}), bf16[128,16,425]{2,1,0:T(8,128)(2,1)}, u32[]{:S(2)}, u32[]{:S(2)}) async-start(bf16[128,16,425]{2,1,0:T(8,128)(2,1)} %pad_maximum_fusion.3), calls=%async_computation.1 | async-start | bytes 4194304 | tf_op jit(solution)/shard_map/all_to_all | solution.py:63
  170.7 1.9 copy-start.15
  170.7 2.2 copy-start.13
  170.7 2.2 copy-start.14
  273.3 2.3 copy-start.4
  297.9 23.0 %all-to-all-start.2 = ((f32[128,1,8]{2,1,0:T(1,128)}), f32[128,1,8]{2,1,0:T(1,128)S(1)}, u32[]{:S(2)}, u32[]{:S(2)}) async-start(f32[128,1,8]{2,1,0:T(1,128)} %broadcast_in_dim.123), calls=%async_computation.2 | async-start | bytes 131072 | tf_op jit(solution)/shard_map/all_to_all | solution.py:190
  323.4 1.6 copy-start.3
  327.1 1.6 copy-start.2
  327.2 1.6 copy-start.7
where the time goes:
time: 336 us; the launch traced here: 332 us
  blocking collectives  135 us (40%)
  waiting for transfers between devices  88.1 us (26%)
  other arithmetic  44 us (13%)
  local copies, waits for them, and re-layouts  22.3 us (7%)
  matrix products  20.2 us (6%)
  starting transfers between devices  19.8 us (6%)
    all_to_all x1, blocking collectives, exchange(): lax.all_to_all(packed, 'img', split_axis=0, concat_axis=0, tiled=True)  116 us
    all_to_all x1, waiting for transfers between devices, exchange(): lax.all_to_all(packed, 'img', split_axis=0, concat_axis=0, tiled=True)  76 us
    psum x1, blocking collectives, body(): score_sum = lax.psum(partial_value, 'vol')  18.7 us
    neg x2, other arithmetic, contrast_of(): return -jnp.sin(defocus * radius.astype(jnp.float32) + phase_shift)  14 us
    all_to_all x1, waiting for transfers between devices, body(): lax.all_to_all(jnp.broadcast_to(pose_weights.reshape(1, 1, -1), (img_coun...  12.1 us
    all_to_all x1, starting transfers between devices, exchange(): lax.all_to_all(packed, 'img', split_axis=0, concat_axis=0, tiled=True)  10 us
    all_to_all x1, starting transfers between devices, body(): lax.all_to_all(jnp.broadcast_to(pose_weights.reshape(1, 1, -1), (img_coun...  9.74 us
  transfers between devices with their start and end apart: 2, of which 2 were waited for; matrix products, arithmetic and copies ran while one was open for 6% of the time, Pallas kernels for 0%

commit v1 on v0

--- a/solution.py
+++ b/solution.py
@@ -183,7 +183,13 @@
     partial_value = jnp.sum(
         (cross_term - 0.5 * power_term).reshape(image_count, pose_count, quarter * size_f), axis=-1
     )
-    score_sum = lax.psum(partial_value, "vol")
+    score_sum = partial_value
+    step = 1
+    while step < vol_count:
+        other = lax.ppermute(score_sum, "vol", [(v, v ^ step) for v in range(vol_count)])
+        lower = (slab_index & step) == 0
+        score_sum = jnp.where(lower, score_sum, other) + jnp.where(lower, other, score_sum)
+        step *= 2
     scores = noise_inv[:, None] * score_sum * (1.0 / math.sqrt(size_k * size_f))
     pose_weights = jax.nn.softmax(scores, axis=-1)
 

time: 336 us -> 335 us (level)
  blocking collectives: 135 us -> 116 us
  starting transfers between devices: 19.8 us -> 29.3 us
  waiting for transfers between devices: 88.1 us -> 94.6 us
    psum x1 -> x0, blocking collectives: 18.7 us -> none  [body(): score_sum = lax.psum(partial_value, 'vol')]
    ppermute x0 -> x2, starting transfers between devices: none -> 10.1 us  [body(): lax.ppermute(score_sum, 'vol', [(v, v ^ step) for v in range(vol_count)])]
    ppermute x0 -> x2, waiting for transfers between devices: none -> 7.07 us  [body(): lax.ppermute(score_sum, 'vol', [(v, v ^ step) for v in range(vol_count)])]
  transfers between devices with their start and end apart: 2 -> 4, of which waited for: 2 -> 4; matrix products, arithmetic and copies ran while one was open for 6% -> 6% of each run, Pallas kernels for 0% -> 0%
where the time goes in v1:
time: 335 us; the launch traced here: 331 us
  blocking collectives  116 us (35%)
  waiting for transfers between devices  94.6 us (28%)
  other arithmetic  45.2 us (13%)
  starting transfers between devices  29.3 us (9%)
  local copies, waits for them, and re-layouts  22.3 us (7%)
  matrix products  20.3 us (6%)
    all_to_all x1, blocking collectives, exchange(): lax.all_to_all(packed, 'img', split_axis=0, concat_axis=0, tiled=True)  116 us
    all_to_all x1, waiting for transfers between devices, exchange(): lax.all_to_all(packed, 'img', split_axis=0, concat_axis=0, tiled=True)  76 us
    neg x2, other arithmetic, contrast_of(): return -jnp.sin(defocus * radius.astype(jnp.float32) + phase_shift)  14 us
    all_to_all x1, waiting for transfers between devices, body(): lax.all_to_all(jnp.broadcast_to(pose_weights.reshape(1, 1, -1), (img_coun...  11.5 us
    ppermute x2, starting transfers between devices, body(): lax.ppermute(score_sum, 'vol', [(v, v ^ step) for v in range(vol_count)])  10.1 us
    all_to_all x1, starting transfers between devices, exchange(): lax.all_to_all(packed, 'img', split_axis=0, concat_axis=0, tiled=True)  10 us
    all_to_all x1, starting transfers between devices, body(): lax.all_to_all(jnp.broadcast_to(pose_weights.reshape(1, 1, -1), (img_coun...  9.17 us
    ppermute x2, waiting for transfers between devices, body(): lax.ppermute(score_sum, 'vol', [(v, v ^ step) for v in range(vol_count)])  7.07 us
  transfers between devices with their start and end apart: 4, of which 4 were waited for; matrix products, arithmetic and copies ran while one was open for 6% of the time, Pallas kernels for 0%

profile of v1, /device:TPU:6, one launch (start us, length us, event | category | flops | bytes accessed | tf_op | source)
XLA Modules:
  0.0 330.8 jit_solution(15239395448119848053)
XLA Ops:
  0.6 0.8 multiply_reduce_fusion
  1.5 1.8 fusion.27
  3.4 3.0 sine_negate_fusion.2
  6.4 3.3 fusion.46
  10.7 0.2 stack_broadcast_in_dim.46
  10.9 0.8 fusion.82
  11.9 0.2 stack_broadcast_in_dim.42
  12.1 0.2 stack_broadcast_in_dim.44
  12.4 0.2 stack_broadcast_in_dim.48
  12.6 0.4 convert_element_type.116
  13.4 0.4 slice_reduce_fusion.4
  13.9 0.5 copy-done.8
  14.5 0.8 fusion.28
  15.3 2.0 fusion.24
  17.3 1.4 copy.53
  18.6 0.6 reshape.294
  19.4 2.5 fusion.16
  21.9 2.7 fusion.9
  24.6 1.4 fusion.21
  26.1 0.5 copy.55
  26.5 2.8 copy.54
  29.3 0.4 pad_maximum_fusion.2
  29.7 116.4 %all_to_all.15 = bf16[128,16,434]{2,1,0:T(8,128)(2,1)S(1)} all-to-all(bf16[128,16,434]{2,1,0:T(8,128)(2,1)S(1)} %pad_maximum_fusion.2), channel_id=1, replica_groups=mesh['img'=128,'vol'=4] {'img'}, dimensions={0} | all-to-all | bytes 3555328 | tf_op jit(solution)/shard_map/all_to_all | solution.py:63
  146.3 0.5 reshape.305
  146.8 0.6 copy-done.1
  147.4 1.3 convert_convert_fusion
  148.7 3.8 %slice_reduce_fusion.1 = (s32[2176]{0:T(1024)S(1)}, s32[2176]{0:T(1024)S(1)}, s32[2176]{0:T(1024)S(1)}, s32[2176]{0:T(1024)S(1)}, s32[2176,1]{1,0:T(8,128)}) fusion(s32[2176,8]{1,0:T(8,128)S(1)} %convert_convert_fusion), kind=kLoop, calls=%fused_computation.59 | loop fusion | flops 10880 | bytes 104448 | tf_op jit(solution)/shard_map/slice | solution.py:155
  152.5 0.8 convolution_convert_fusion
  153.5 1.2 copy.62
  154.8 2.4 copy.61
  157.2 3.5 %pad_maximum_fusion.3 = bf16[128,16,425]{2,1,0:T(8,128)(2,1)} fusion(bf16[128,16,25]{2,1,0:T(8,128)(2,1)} %copy.62, bf16[128,16,400]{2,1,0:T(8,128)(2,1)} %bitcast.67), kind=kLoop, calls=%fused_computation.31 | loop fusion | flops 3481600 | bytes 3481600 | tf_op jit(solution)/shard_map/concatenate | solution.py:62
  160.7 10.0 %all-to-all-start.1 = ((bf16[128,16,425]{2,1,0:T(8,128)(2,1)}), bf16[128,16,425]{2,1,0:T(8,128)(2,1)}, u32[]{:S(2)}, u32[]{:S(2)}) async-start(bf16[128,16,425]{2,1,0:T(8,128)(2,1)} %pad_maximum_fusion.3), calls=%async_computation.1 | async-start | bytes 4194304 | tf_op jit(solution)/shard_map/all_to_all | solution.py:63
  170.8 1.2 convert_element_type.135
  172.9 0.7 fusion.88
  173.6 4.7 %sine_negate_fusion.1 = f32[800,200]{0,1:T(8,128)} fusion(f32[]{:T(128)} %get-tuple-element.29, s32[200]{0:T(256)S(1)} %iota_multiply_fusion, s32[800]{0:T(1024)S(1)} %add.157, f32[]{:T(128)} %get-tuple-element.28), kind=kLoop, calls=%fused_computation.94 | loop fusion | flops 800000 | bytes 644008 | tf_op jit(solution)/shard_map/neg | solution.py:27
  178.3 1.6 slice_reduce_fusion.2
  180.0 1.0 slice_reduce_fusion.5
  181.3 9.3 %sine_negate_fusion = f32[2176,200]{1,0:T(8,128)} fusion(f32[2176]{0:T(1024)S(1)} %get-tuple-element.16, s32[200]{0:T(256)S(1)} %iota_multiply_fusion, s32[2176]{0:T(1024)S(1)} %get-tuple-element.10, f32[2176]{0:T(1024)S(1)} %get-tuple-element.15), kind=kLoop, calls=%fused_computation.26 | loop fusion | flops 2176000 | bytes 1767712 | tf_op jit(solution)/shard_map/neg | solution.py:27
  190.6 76.0 %all-to-all-done.1 = bf16[128,16,425]{2,1,0:T(8,128)(2,1)} async-done(((bf16[128,16,425]{2,1,0:T(8,128)(2,1)}), bf16[128,16,425]{2,1,0:T(8,128)(2,1)}, u32[]{:S(2)}, u32[]{:S(2)}) %all-to-all-start.1) | async-done | bytes 1740832 | tf_op jit(solution)/shard_map/all_to_all | solution.py:63
  266.6 1.2 slice.145
  267.9 1.2 reshape.306
  269.0 2.0 pad_maximum_fusion.1
  271.0 2.3 fusion.25
  273.3 2.3 multiply_add_fusion
  275.6 0.3 fusion.56
  276.1 1.9 collective-permute-start
  278.0 1.1 collective-permute-done
  279.1 8.2 %collective-permute-start.1 = (f32[1,8]{1,0:T(1,128)S(1)}, f32[1,8]{1,0:T(1,128)S(1)}, u32[]{:S(2)}, u32[]{:S(2)}) collective-permute-start(f32[1,8]{1,0:T(1,128)S(1)} %fusion.87), channel_id=1, source_target_pairs={{0,2},{1,3},{2,0},{3,1},{4,6},{5,7},{6,4},{7,5},{8,10},{9,11},{10,... | collective-permute-start | bytes 104 | tf_op jit(solution)/shard_map/ppermute | solution.py:189
  287.3 5.9 %collective-permute-done.1 = f32[1,8]{1,0:T(1,128)S(1)} collective-permute-done((f32[1,8]{1,0:T(1,128)S(1)}, f32[1,8]{1,0:T(1,128)S(1)}, u32[]{:S(2)}, u32[]{:S(2)}) %collective-permute-start.1) | collective-permute-done | bytes 64 | tf_op jit(solution)/shard_map/ppermute | solution.py:189
  293.3 0.6 fusion.102
  293.9 1.2 fusion.101
  295.1 1.2 fusion.109
  296.4 0.7 broadcast_in_dim.123
  297.0 9.2 %all-to-all-start.2 = ((f32[128,1,8]{2,1,0:T(1,128)}), f32[128,1,8]{2,1,0:T(1,128)S(1)}, u32[]{:S(2)}, u32[]{:S(2)}) async-start(f32[128,1,8]{2,1,0:T(1,128)} %broadcast_in_dim.123), calls=%async_computation.2 | async-start | bytes 131072 | tf_op jit(solution)/shard_map/all_to_all | solution.py:196
  306.2 1.7 broadcast_divide_fusion
  308.0 11.5 %all-to-all-done.2 = f32[128,1,8]{2,1,0:T(1,128)S(1)} async-done(((f32[128,1,8]{2,1,0:T(1,128)}), f32[128,1,8]{2,1,0:T(1,128)S(1)}, u32[]{:S(2)}, u32[]{:S(2)}) %all-to-all-start.2) | async-done | bytes 4128 | tf_op jit(solution)/shard_map/all_to_all | solution.py:196
  319.7 1.8 fusion.81
  321.6 0.4 copy.67
  322.0 1.0 fusion.35
  323.0 0.7 copy-done.3
  323.7 2.1 fusion.33
  325.7 0.4 broadcast_multiply_fusion
  326.1 1.2 copy-done.2
  327.3 3.2 fusion.30
  (69 shorter events, 3.1 us)
Async XLA Ops:
  0.6 13.3 %copy-start = (bf16[1,400,400]{2,1,0:T(8,128)(2,1)S(1)}, bf16[1,400,400]{2,1,0:T(8,128)(2,1)}, u32[]{:S(2)}) copy-start(bf16[1,400,400]{2,1,0:T(8,128)(2,1)} %param.11) | copy-start | bytes 960004
  3.3 7.1 %copy-start.11 = (s32[1,1,8,100]{3,2,1,0:T(8,128)S(1)}, s32[1,1,8,100]{3,2,1,0:T(8,128)}, u32[]{:S(2)}) copy-start(s32[1,1,8,100]{3,2,1,0:T(8,128)} %param.16) | copy-start | bytes 9604
  3.3 7.1 %copy-start.12 = (s32[1,1,8,200]{3,2,1,0:T(8,128)S(1)}, s32[1,1,8,200]{3,2,1,0:T(8,128)}, u32[]{:S(2)}) copy-start(s32[1,1,8,200]{3,2,1,0:T(8,128)} %param.15) | copy-start | bytes 19204
  13.3 1.0 copy-start.8
  13.4 1.1 copy-start.9
  19.3 2.7 copy-start.5
  146.1 1.3 copy-start.1
  146.8 5.7 %copy-start.6 = (bf16[128,416]{1,0:T(8,128)(2,1)}, bf16[128,416]{1,0:T(8,128)(2,1)S(1)}, u32[]{:S(2)}) copy-start(bf16[128,416]{1,0:T(8,128)(2,1)S(1)} %reshape.305) | copy-start | bytes 319492
  148.7 3.8 %copy-start.10 = (bf16[1,256,400]{1,2,0:T(8,128)(2,1)S(1)}, bf16[1,256,400]{1,2,0:T(8,128)(2,1)}, u32[]{:S(2)}) copy-start(bf16[1,256,400]{1,2,0:T(8,128)(2,1)} %param.12) | copy-start | bytes 614404
  160.7 105.9 %all-to-all-start.1 = ((bf16[128,16,425]{2,1,0:T(8,128)(2,1)}), bf16[128,16,425]{2,1,0:T(8,128)(2,1)}, u32[]{:S(2)}, u32[]{:S(2)}) async-start(bf16[128,16,425]{2,1,0:T(8,128)(2,1)} %pad_maximum_fusion.3), calls=%async_computation.1 | async-start | bytes 4194304 | tf_op jit(solution)/shard_map/all_to_all | solution.py:63
  170.7 1.9 copy-start.15
  170.7 2.2 copy-start.13
  170.7 2.2 copy-start.14
  273.3 2.3 copy-start.4
  276.1 3.0 collective-permute-start
  279.1 14.2 %collective-permute-start.1 = (f32[1,8]{1,0:T(1,128)S(1)}, f32[1,8]{1,0:T(1,128)S(1)}, u32[]{:S(2)}, u32[]{:S(2)}) collective-permute-start(f32[1,8]{1,0:T(1,128)S(1)} %fusion.87), channel_id=1, source_target_pairs={{0,2},{1,3},{2,0},{3,1},{4,6},{5,7},{6,4},{7,5},{8,10},{9,11},{10,... | collective-permute-start | bytes 104 | tf_op jit(solution)/shard_map/ppermute | solution.py:189
  297.0 22.4 %all-to-all-start.2 = ((f32[128,1,8]{2,1,0:T(1,128)}), f32[128,1,8]{2,1,0:T(1,128)S(1)}, u32[]{:S(2)}, u32[]{:S(2)}) async-start(f32[128,1,8]{2,1,0:T(1,128)} %broadcast_in_dim.123), calls=%async_computation.2 | async-start | bytes 131072 | tf_op jit(solution)/shard_map/all_to_all | solution.py:196
  322.0 1.6 copy-start.3
  325.7 1.6 copy-start.2
  325.7 1.6 copy-start.7
